TPU v7x, 32 devices: a whole 2x2x4 slice. The times are simulated.
32 devices in a mesh: rep: 2 (over y), grp: 4 (over z), sub: 4 (over x, core).
Axes of the slice: x: 2, y: 2, z: 4, core: 2. Of those that a mesh axis runs over, the one named last changes fastest.
Arguments:
- volume: bfloat16 [256, 8, 8, 128], P(None, ('rep', 'grp'), 'sub'), parts along dimension 1, may hold values from -6 to 6
- cotangent: bfloat16 [256, 8, 8, 128], P(None, ('rep', 'grp'), 'sub'), parts along dimension 1, may hold values from -6 to 6
- first_weight: bfloat16 [256, 256], replicated, may hold values from -0.375 to 0.375
- group_weight: bfloat16 [256, 8, 3, 3, 3], replicated, may hold values from -0.4375 to 0.4375
- third_weight: bfloat16 [256, 256], replicated, may hold values from -0.375 to 0.375
Outputs:
- block_output: bfloat16 [256, 8, 8, 128], P(None, ('rep', 'grp'), 'sub'), parts along dimension 1
- volume_grad: bfloat16 [256, 8, 8, 128], P(None, ('rep', 'grp'), 'sub'), parts along dimension 1
- first_grad: float32 [512, 256], P('rep'), parts along dimension 0
- group_grad: float32 [512, 8, 3, 3, 3], P(('rep', 'grp')), parts along dimension 0
- third_grad: float32 [512, 256], P('rep'), parts along dimension 0
There are 2 independent parts, one for each index of `rep`. A program takes and returns all parts, laid end to end along the dimension named above; an argument that names none is the same for every part. Nothing has to cross between parts.
All inputs are finite; a program needn't handle non-finite values.
Results may differ from a plain program's by a relative error of at most 0.0073.
Values may be sent and summed in bfloat16 or wider, within the bound.
No kernel may reach another device: no remote copies, remote signals or barrier semaphores. Data moves between devices by JAX's collectives and lax.ppermute only.
A program may use at most 64 MiB of HBM per device.

v0:
```python
import math
import jax
import jax.numpy as jnp
from jax import lax
from jax.sharding import PartitionSpec as P

GW = 8


def padded_2(block, sides, width):
    for axis, dim in sides:
        count = lax.axis_size(axis)
        forward = [(i, i + 1) for i in range(count - 1)]
        backward = [(target, source) for source, target in forward]
        low = lax.ppermute(
            lax.slice_in_dim(block, block.shape[dim] - width, None, axis=dim), axis, forward
        )
        high = lax.ppermute(lax.slice_in_dim(block, 0, width, axis=dim), axis, backward)
        block = jnp.concatenate([low, block, high], axis=dim)
    return block


def silu_slope(values):
    sigma = jax.nn.sigmoid(values)
    return sigma * (1.0 + values * (1.0 - sigma))


def dense_conv(source, kernel, depth_pad):
    padding = ((depth_pad, depth_pad), (0, 0), (1, 1))
    return lax.conv_general_dilated(
        source[None],
        kernel,
        (1, 1, 1),
        padding,
        dimension_numbers=("NCDHW", "OIDHW", "NCDHW"),
        preferred_element_type=jnp.float32,
    )[0]


def block_diagonal(kernel):
    rows = kernel.shape[0]
    tiled = jnp.tile(kernel, (1, rows // GW, 1, 1, 1))
    group_of = jnp.arange(rows) // GW
    mask = (group_of[:, None] == group_of[None, :]).astype(kernel.dtype)
    return tiled * mask[:, :, None, None, None]


def diagonal_blocks(dense):
    rows = dense.shape[1]
    groups = rows // GW
    shaped = dense.reshape(groups, GW, rows, *dense.shape[2:])
    group_of = jnp.arange(rows) // GW
    mask = (jnp.arange(groups)[:, None] == group_of[None, :]).astype(dense.dtype)
    picked = (shaped * mask[:, None, :, None, None, None]).sum(axis=0)
    return picked.transpose(1, 0, 2, 3, 4)


def weight_grad(padded, deltas):
    return lax.conv_general_dilated(
        padded[None],
        deltas[None],
        (1, 1, 1),
        "VALID",
        dimension_numbers=("CNDHW", "IODHW", "NCDHW"),
        preferred_element_type=jnp.float32,
    )


def per_device(volume, cotangent, first_weight, group_weight, third_weight):
    channels, depth, height, width = volume.shape
    flattened = volume.reshape(channels, -1)
    contract_lead = (((0,), (0,)), ((), ()))
    contract_tail = (((1,), (1,)), ((), ()))
    total_cells = depth * lax.axis_size("grp") * height * lax.axis_size("sub") * width
    factor = 1.0 / math.sqrt(total_cells)
    group_rows = channels // lax.axis_size("grp")
    first_pre = lax.dot_general(
        first_weight, flattened, contract_lead, preferred_element_type=jnp.float32
    )
    first_act = jax.nn.silu(first_pre).astype(jnp.bfloat16).reshape(volume.shape)
    own_kernel = lax.dynamic_slice_in_dim(
        group_weight, lax.axis_index("grp") * group_rows, group_rows, 0
    )
    dense_kernel = block_diagonal(own_kernel)
    gathered = lax.all_to_all(first_act, "grp", split_axis=0, concat_axis=1, tiled=True)
    padded_act = padded_2(gathered, (("sub", 2),), 1)
    group_pre = dense_conv(padded_act, dense_kernel, 1)
    group_act = jax.nn.silu(group_pre).astype(jnp.bfloat16)
    returned = lax.all_to_all(group_act, "grp", split_axis=1, concat_axis=0, tiled=True)
    act_flat = returned.reshape(channels, -1)
    summed = flattened.astype(jnp.float32) + lax.dot_general(
        third_weight, act_flat, contract_lead, preferred_element_type=jnp.float32
    )
    block_output = jax.nn.silu(summed).astype(jnp.bfloat16).reshape(volume.shape)
    third_delta = (cotangent.reshape(channels, -1).astype(jnp.float32) * silu_slope(summed)).astype(
        jnp.bfloat16
    )
    third_part = lax.dot_general(
        act_flat, third_delta, contract_tail, preferred_element_type=jnp.float32
    )
    third_grad = lax.psum(third_part, ("grp", "sub")) * factor
    hidden_grad = (
        jnp.dot(third_weight, third_delta, preferred_element_type=jnp.float32)
        .astype(jnp.bfloat16)
        .reshape(volume.shape)
    )
    arriving = lax.all_to_all(hidden_grad, "grp", split_axis=0, concat_axis=1, tiled=True)
    group_delta = (arriving.astype(jnp.float32) * silu_slope(group_pre)).astype(jnp.bfloat16)
    delta_rim = padded_2(group_delta, (("sub", 2),), 1)
    flipped = dense_kernel.transpose(1, 0, 2, 3, 4)[:, :, ::-1, ::-1, ::-1]
    inner_local = dense_conv(delta_rim, flipped, 1).astype(jnp.bfloat16)
    dense_grad = weight_grad(jnp.pad(padded_act, ((0, 0), (1, 1), (0, 0), (1, 1))), group_delta)
    kernel_part = diagonal_blocks(dense_grad)
    inner_grad = lax.all_to_all(inner_local, "grp", split_axis=1, concat_axis=0, tiled=True)
    group_grad = lax.psum(kernel_part, "sub") * factor
    first_delta = (
        inner_grad.reshape(channels, -1).astype(jnp.float32) * silu_slope(first_pre)
    ).astype(jnp.bfloat16)
    first_part = lax.dot_general(
        flattened, first_delta, contract_tail, preferred_element_type=jnp.float32
    )
    volume_grad = (
        (
            third_delta.astype(jnp.float32)
            + jnp.dot(first_weight, first_delta, preferred_element_type=jnp.float32)
        )
        .astype(jnp.bfloat16)
        .reshape(volume.shape)
    )
    first_grad = lax.psum(first_part, ("grp", "sub")) * factor
    return (block_output, volume_grad, first_grad, group_grad, third_grad)


def solution(mesh):
    in_specs = (
        P(None, ("rep", "grp"), "sub", None),
        P(None, ("rep", "grp"), "sub", None),
        P(),
        P(),
        P(),
    )
    out_specs = (
        P(None, ("rep", "grp"), "sub", None),
        P(None, ("rep", "grp"), "sub", None),
        P("rep", None),
        P(("rep", "grp"), None, None, None, None),
        P("rep", None),
    )
    return jax.shard_map(
        per_device, mesh=mesh, in_specs=in_specs, out_specs=out_specs, check_vma=False
    )
```

profile of v0, /device:TPU:1, one launch (start us, length us, event | category | flops | bytes accessed | tf_op | source)
XLA Modules:
  0.0 194.1 jit_solution(14904769792690059259)
XLA Ops:
  7.2 0.0 copy-start
  7.2 1.0 copy.70
  8.2 0.0 copy-start.4
  8.2 1.8 multiply_convert_fusion.2
  10.1 0.8 copy.71
  10.9 5.4 %all-to-all-start = ((bf16[256,1,2,128]{3,2,1,0:T(2,128)(2,1)}), bf16[256,1,2,128]{3,2,1,0:T(2,128)(2,1)S(1)}, u32[]{:S(2)}, u32[]{:S(2)}) async-start(bf16[256,1,2,128]{3,2,1,0:T(2,128)(2,1)} %copy.71), calls=%async_computation | async-start | bytes 262144 | tf_op jit(solution)/shard_map/all_to_all | solution.py:85
  16.3 0.1 compare_convert_fusion
  16.4 4.7 %all-to-all-done = bf16[256,1,2,128]{3,2,1,0:T(2,128)(2,1)S(1)} async-done(((bf16[256,1,2,128]{3,2,1,0:T(2,128)(2,1)}), bf16[256,1,2,128]{3,2,1,0:T(2,128)(2,1)S(1)}, u32[]{:S(2)}, u32[]{:S(2)}) %all-to-all-start) | async-done | bytes 131104 | tf_op jit(solution)/shard_map/all_to_all | solution.py:85
  21.1 5.2 %collective-permute-start = (bf16[64,4,1,128]{3,0,1,2:T(8,128)(2,1)S(1)}, bf16[64,4,1,128]{3,0,1,2:T(8,128)(2,1)S(1)}, u32[]{:S(2)}, u32[]{:S(2)}) collective-permute-start(bf16[64,4,1,128]{3,0,1,2:T(8,128)(2,1)S(1)} %get-tuple-element.33), channel_id=1, source_target_pairs={{0,1},{1,2},{2,3},{4,5},{5,6},{6,7},{8,9},{9,10},{10,11},{12,13},{... | collective-permute-start | bytes 196616 | tf_op jit(solution)/shard_map/ppermute | solution.py:15
  26.4 1.9 collective-permute-start.1
  28.3 0.1 constant_dynamic-slice_fusion
  28.4 3.5 %collective-permute-done.1 = bf16[64,4,1,128]{3,0,1,2:T(8,128)(2,1)S(1)} collective-permute-done((bf16[64,4,1,128]{3,0,1,2:T(8,128)(2,1)S(1)}, bf16[64,4,1,128]{3,0,1,2:T(8,128)(2,1)S(1)}, u32[]{:S(2)}, u32[]{:S(2)}) %collective-permute-start.1) | collective-permute-done | bytes 65568 | tf_op jit(solution)/shard_map/ppermute | solution.py:18
  32.0 0.3 copy.107
  32.3 0.0 copy-start.5
  32.3 0.3 pad.5.clone
  32.6 0.1 copy.75
  32.7 0.3 copy-done.5
  33.0 1.2 add_multiply_fusion
  34.2 0.3 copy.76
  34.6 0.2 copy.105
  34.8 0.7 fusion.28
  35.5 3.3 %all-to-all-start.1 = ((bf16[64,4,2,128]{3,0,2,1:T(8,128)(2,1)}), bf16[64,4,2,128]{3,0,2,1:T(8,128)(2,1)S(1)}, u32[]{:S(2)}, u32[]{:S(2)}) async-start(bf16[64,4,2,128]{3,0,2,1:T(8,128)(2,1)} %fusion.28), calls=%async_computation.1 | async-start | bytes 262144 | tf_op jit(solution)/shard_map/all_to_all | solution.py:89
  38.9 0.8 copy.79
  39.7 0.3 copy.91
  40.0 0.2 copy.106
  40.2 0.2 pad_bitcast_fusion
  40.5 1.7 copy.93
  42.2 1.4 all-to-all-done.1
  43.6 0.1 copy.78
  43.7 1.3 fusion.24
  45.0 0.2 convolution_convert_fusion
  45.2 0.8 copy.80
  46.0 3.3 %all-to-all-start.2 = ((bf16[256,1,2,128]{3,2,1,0:T(2,128)(2,1)}), bf16[256,1,2,128]{3,2,1,0:T(2,128)(2,1)S(1)}, u32[]{:S(2)}, u32[]{:S(2)}) async-start(bf16[256,1,2,128]{3,2,1,0:T(2,128)(2,1)} %copy.80), calls=%async_computation.2 | async-start | bytes 262144 | tf_op jit(solution)/shard_map/all_to_all | solution.py:107
  49.4 0.8 copy.96
  50.1 0.9 fusion.35
  51.1 3.5 %all-to-all-done.2 = bf16[256,1,2,128]{3,2,1,0:T(2,128)(2,1)S(1)} async-done(((bf16[256,1,2,128]{3,2,1,0:T(2,128)(2,1)}), bf16[256,1,2,128]{3,2,1,0:T(2,128)(2,1)S(1)}, u32[]{:S(2)}, u32[]{:S(2)}) %all-to-all-start.2) | async-done | bytes 131104 | tf_op jit(solution)/shard_map/all_to_all | solution.py:107
  54.6 0.1 fusion.23
  54.8 3.7 %collective-permute-start.2 = (bf16[64,4,1,128]{3,0,2,1:T(8,128)(2,1)S(1)}, bf16[64,4,1,128]{3,0,2,1:T(8,128)(2,1)S(1)}, u32[]{:S(2)}, u32[]{:S(2)}) collective-permute-start(bf16[64,4,1,128]{3,0,2,1:T(8,128)(2,1)S(1)} %get-tuple-element.31), channel_id=1, source_target_pairs={{0,1},{1,2},{2,3},{4,5},{5,6},{6,7},{8,9},{9,10},{10,11},{12,13},{... | collective-permute-start | bytes 196616 | tf_op jit(solution)/shard_map/ppermute | solution.py:15
  58.4 1.9 collective-permute-start.3
  60.4 0.4 copy.94
  60.8 3.2 %collective-permute-done.3 = bf16[64,4,1,128]{3,0,2,1:T(8,128)(2,1)S(1)} collective-permute-done((bf16[64,4,1,128]{3,0,2,1:T(8,128)(2,1)S(1)}, bf16[64,4,1,128]{3,0,2,1:T(8,128)(2,1)S(1)}, u32[]{:S(2)}, u32[]{:S(2)}) %collective-permute-start.3) | collective-permute-done | bytes 65568 | tf_op jit(solution)/shard_map/ppermute | solution.py:18
  64.1 0.3 copy.108
  64.4 0.3 pad.7.clone
  64.7 0.1 copy.85
  64.8 2.1 %fusion.4 = bf16[4,2,8,17,64]{4,2,3,1,0:T(8,128)(2,1)S(1)} fusion(bf16[64,4,4,1,7,2]{0,4,5,2,1,3:T(8,128)(2,1)S(1)} %slice.27, bf16[64,4,4,1,8,17]{0,4,5,2,1,3:T(8,128)(2,1)S(1)} %copy.85, pred[8,17]{0,1:T(8,128)(4,1)S(1)} %copy-done.5, bf16[64,64]{0,1:T(8,128)(2,1)S(1)} %compare_convert_fusion, bf16[64,8,3,3,3]{0,1,4,3,2:T(8,128)(2,1)S(1)} %constant_dynamic-slice_fusion), kind=kOutput, calls=%fused_computation.8 | convolution fusion | flops 202055680 | bytes 482440 | tf_op jit(solution)/shard_map/conv_general_dilated | solution.py:30
  66.9 0.2 copy.86
  67.1 0.2 slice_bitcast_fusion
  67.3 0.8 copy.87
  68.1 3.3 %all-to-all-start.3 = ((bf16[64,4,2,128]{3,0,2,1:T(8,128)(2,1)}), bf16[64,4,2,128]{3,0,2,1:T(8,128)(2,1)S(1)}, u32[]{:S(2)}, u32[]{:S(2)}) async-start(bf16[64,4,2,128]{3,0,2,1:T(8,128)(2,1)} %copy.87), calls=%async_computation.3 | async-start | bytes 262144 | tf_op jit(solution)/shard_map/all_to_all | solution.py:114
  71.4 0.2 all-reduce.4.cloned.1.call-start
  71.7 7.9 %fusion.3 = f32[8,64,3,3,3]{1,0,4,3,2:T(8,128)S(1)} fusion(bf16[1,64,6,4,130]{1,0,4,3,2:T(2,128)(2,1)S(1)} %copy.93, bf16[1,64,4,2,128]{1,0,4,3,2:T(2,128)(2,1)S(1)} %copy.94, f32[8,64]{1,0:T(8,128)S(1)} %fusion.40), kind=kOutput, calls=%fused_computation.7 | convolution fusion | flops 226699776 | bytes 587776 | tf_op jit(solution)/shard_map/conv_general_dilated | solution.py:59
  79.6 11.5 %psum.22 = f32[64,8,3,3,3]{0,1,4,3,2:T(8,128)S(1)} all-reduce(f32[64,8,3,3,3]{0,1,4,3,2:T(8,128)S(1)} %bitcast.154), channel_id=1, replica_groups=mesh['rep'=2,'grp'=4,'sub'=4] {'sub'}, use_global_device_ids=true, to_apply=%region_2.3 | all-reduce | flops 13824 | bytes 110592 | tf_op jit(solution)/shard_map/psum | solution.py:115
  91.2 0.2 copy.101
  91.4 0.3 reshape.178
  91.8 0.1 multiply_convert_fusion
  91.9 0.9 convolution_bitcast_fusion.1
  92.8 0.0 all-reduce.4.cloned.1.call-update
  92.9 0.7 broadcast_multiply_fusion.2
  93.5 0.2 fusion.7
  93.7 0.8 copy.97
  94.5 89.9 %all-reduce.4.cloned.1.call-done = (f32[256,256]{0,1:T(8,128)}, f32[256,256]{0,1:T(8,128)}) async-done(((f32[256,256]{0,1:T(8,128)}, f32[256,256]{0,1:T(8,128)}), (f32[256,256]{0,1:T(8,128)}, f32[256,256]{0,1:T(8,128)})) %all-reduce.4.cloned.1.call-update) | async-done | bytes 524304 | tf_op jit(solution)/shard_map/psum | solution.py:130
  184.5 1.1 broadcast_multiply_fusion
  185.5 0.8 copy.98
  186.4 0.8 copy.99
  (25 shorter events, 0.3 us)
Async XLA Ops:
  7.2 36.6 %copy-start = (bf16[256,256]{1,0:T(8,128)(2,1)S(1)}, bf16[256,256]{1,0:T(8,128)(2,1)}, u32[]{:S(2)}) copy-start(bf16[256,256]{1,0:T(8,128)(2,1)} %param.9) | copy-start | bytes 393220
  8.2 20.1 %copy-start.4 = (bf16[256,8,3,3,3]{0,1,4,3,2:T(8,128)(2,1)S(1)}, bf16[256,8,3,3,3]{0,1,4,3,2:T(8,128)(2,1)}, u32[]{:S(2)}) copy-start(bf16[256,8,3,3,3]{0,1,4,3,2:T(8,128)(2,1)} %param.8) | copy-start | bytes 331780
  10.9 10.2 %all-to-all-start = ((bf16[256,1,2,128]{3,2,1,0:T(2,128)(2,1)}), bf16[256,1,2,128]{3,2,1,0:T(2,128)(2,1)S(1)}, u32[]{:S(2)}, u32[]{:S(2)}) async-start(bf16[256,1,2,128]{3,2,1,0:T(2,128)(2,1)} %copy.71), calls=%async_computation | async-start | bytes 262144 | tf_op jit(solution)/shard_map/all_to_all | solution.py:85
  21.1 7.3 %collective-permute-start = (bf16[64,4,1,128]{3,0,1,2:T(8,128)(2,1)S(1)}, bf16[64,4,1,128]{3,0,1,2:T(8,128)(2,1)S(1)}, u32[]{:S(2)}, u32[]{:S(2)}) collective-permute-start(bf16[64,4,1,128]{3,0,1,2:T(8,128)(2,1)S(1)} %get-tuple-element.33), channel_id=1, source_target_pairs={{0,1},{1,2},{2,3},{4,5},{5,6},{6,7},{8,9},{9,10},{10,11},{12,13},{... | collective-permute-start | bytes 196616 | tf_op jit(solution)/shard_map/ppermute | solution.py:15
  26.4 5.6 %collective-permute-start.1 = (bf16[64,4,1,128]{3,0,1,2:T(8,128)(2,1)S(1)}, bf16[64,4,1,128]{3,0,1,2:T(8,128)(2,1)S(1)}, u32[]{:S(2)}, u32[]{:S(2)}) collective-permute-start(bf16[64,4,1,128]{3,0,1,2:T(8,128)(2,1)S(1)} %get-tuple-element.34), channel_id=1, source_target_pairs={{1,0},{2,1},{3,2},{5,4},{6,5},{7,6},{9,8},{10,9},{11,10},{13,12},{... | collective-permute-start | bytes 196616 | tf_op jit(solution)/shard_map/ppermute | solution.py:18
  32.3 0.7 copy-start.5
  34.5 4.3 %copy-start.2 = (bf16[256,1,2,128]{3,2,1,0:T(2,128)(2,1)S(1)}, bf16[256,1,2,128]{3,2,1,0:T(2,128)(2,1)}, u32[]{:S(2)}) copy-start(bf16[256,1,2,128]{3,2,1,0:T(2,128)(2,1)} %param.6) | copy-start | bytes 393220
  35.5 8.1 %all-to-all-start.1 = ((bf16[64,4,2,128]{3,0,2,1:T(8,128)(2,1)}), bf16[64,4,2,128]{3,0,2,1:T(8,128)(2,1)S(1)}, u32[]{:S(2)}, u32[]{:S(2)}) async-start(bf16[64,4,2,128]{3,0,2,1:T(8,128)(2,1)} %fusion.28), calls=%async_computation.1 | async-start | bytes 262144 | tf_op jit(solution)/shard_map/all_to_all | solution.py:89
  46.0 8.6 %all-to-all-start.2 = ((bf16[256,1,2,128]{3,2,1,0:T(2,128)(2,1)}), bf16[256,1,2,128]{3,2,1,0:T(2,128)(2,1)S(1)}, u32[]{:S(2)}, u32[]{:S(2)}) async-start(bf16[256,1,2,128]{3,2,1,0:T(2,128)(2,1)} %copy.80), calls=%async_computation.2 | async-start | bytes 262144 | tf_op jit(solution)/shard_map/all_to_all | solution.py:107
  54.8 6.0 %collective-permute-start.2 = (bf16[64,4,1,128]{3,0,2,1:T(8,128)(2,1)S(1)}, bf16[64,4,1,128]{3,0,2,1:T(8,128)(2,1)S(1)}, u32[]{:S(2)}, u32[]{:S(2)}) collective-permute-start(bf16[64,4,1,128]{3,0,2,1:T(8,128)(2,1)S(1)} %get-tuple-element.31), channel_id=1, source_target_pairs={{0,1},{1,2},{2,3},{4,5},{5,6},{6,7},{8,9},{9,10},{10,11},{12,13},{... | collective-permute-start | bytes 196616 | tf_op jit(solution)/shard_map/ppermute | solution.py:15
  58.4 5.6 %collective-permute-start.3 = (bf16[64,4,1,128]{3,0,2,1:T(8,128)(2,1)S(1)}, bf16[64,4,1,128]{3,0,2,1:T(8,128)(2,1)S(1)}, u32[]{:S(2)}, u32[]{:S(2)}) collective-permute-start(bf16[64,4,1,128]{3,0,2,1:T(8,128)(2,1)S(1)} %get-tuple-element.32), channel_id=1, source_target_pairs={{1,0},{2,1},{3,2},{5,4},{6,5},{7,6},{9,8},{10,9},{11,10},{13,12},{... | collective-permute-start | bytes 196616 | tf_op jit(solution)/shard_map/ppermute | solution.py:18
  68.1 23.1 %all-to-all-start.3 = ((bf16[64,4,2,128]{3,0,2,1:T(8,128)(2,1)}), bf16[64,4,2,128]{3,0,2,1:T(8,128)(2,1)S(1)}, u32[]{:S(2)}, u32[]{:S(2)}) async-start(bf16[64,4,2,128]{3,0,2,1:T(8,128)(2,1)} %copy.87), calls=%async_computation.3 | async-start | bytes 262144 | tf_op jit(solution)/shard_map/all_to_all | solution.py:114
  71.4 113.0 %all-reduce.4.cloned.1.call-start = ((), (), s32[]{:S(2)}) async-start(), calls=%async_computation.4 | async-start | bytes 1048576 | tf_op jit(solution)/shard_map/psum | solution.py:130
  79.6 12.2 %copy-start.1 = (f32[256,256]{0,1:T(8,128)S(1)}, f32[256,256]{0,1:T(8,128)}, u32[]{:S(2)}) copy-start(f32[256,256]{0,1:T(8,128)} %get-tuple-element.36) | copy-start | bytes 786436
  91.4 2.1 %copy-start.3 = (bf16[256,256]{1,0:T(8,128)(2,1)S(1)}, bf16[256,256]{1,0:T(8,128)(2,1)}, u32[]{:S(2)}) copy-start(bf16[256,256]{1,0:T(8,128)(2,1)} %param.7) | copy-start | bytes 393220
Sparse Core Ops, SparseCore 0:
  93.0 91.4 all-reduce.3
where the time goes:
time: 195 us; the launch traced here: 194 us
  waiting for transfers between devices  106 us (54%)
  starting transfers between devices  28.3 us (15%)
  matrix products  16.7 us (9%)
  between operations  14.5 us (7%)
  local copies, waits for them, and re-layouts  13.7 us (7%)
  blocking collectives  11.5 us (6%)
  other arithmetic  2.91 us (1%)
    psum x1, waiting for transfers between devices, per_device(): first_grad = lax.psum(first_part, ('grp', 'sub')) * factor  89.9 us
    psum x1, blocking collectives, per_device(): group_grad = lax.psum(kernel_part, 'sub') * factor  11.5 us
    ppermute x2, starting transfers between devices, padded_2(): lax.ppermute(lax.slice_in_dim(block, block.shape[dim] - width, None, axis...  8.89 us
    conv_general_dilated x1, matrix products, weight_grad(): lax.conv_general_dilated(padded[None], deltas[None], (1, 1, 1), 'VALID',...  7.92 us
    ppermute x2, waiting for transfers between devices, padded_2(): lax.ppermute(lax.slice_in_dim(block, 0, width, axis=dim), axis, backward)  6.74 us
    unnamed x21, local copies, waits for them, and re-layouts  5.57 us
    all_to_all x1, starting transfers between devices, per_device(): lax.all_to_all(first_act, 'grp', split_axis=0, concat_axis=1, tiled=True)  5.42 us
    all_to_all x1, waiting for transfers between devices, per_device(): lax.all_to_all(first_act, 'grp', split_axis=0, concat_axis=1, tiled=True)  4.73 us
  transfers between devices with their start and end apart: 9, of which 6 were waited for; matrix products, arithmetic and copies ran while one was open for 8% of the time, Pallas kernels for 0%

commit v1 on v0

--- a/solution.py
+++ b/solution.py
@@ -112,7 +112,7 @@
     dense_grad = weight_grad(jnp.pad(padded_act, ((0, 0), (1, 1), (0, 0), (1, 1))), group_delta)
     kernel_part = diagonal_blocks(dense_grad)
     inner_grad = lax.all_to_all(inner_local, "grp", split_axis=1, concat_axis=0, tiled=True)
-    group_grad = lax.psum(kernel_part, "sub") * factor
+    group_grad = jnp.sum(lax.all_gather(kernel_part, "sub"), axis=0) * factor
     first_delta = (
         inner_grad.reshape(channels, -1).astype(jnp.float32) * silu_slope(first_pre)
     ).astype(jnp.bfloat16)

time: 195 us -> 219 us (1.12)
  blocking collectives: 11.5 us -> 28.8 us
  other arithmetic: 2.91 us -> 7.21 us
    all_gather x0 -> x1, blocking collectives: none -> 28.8 us  [per_device(): group_grad = jnp.sum(lax.all_gather(kernel_part, 'sub'), axis=0) * factor]
    psum x1 -> x0, blocking collectives: 11.5 us -> none  [per_device(): group_grad = lax.psum(kernel_part, 'sub') * factor]
    reduce_sum x0 -> x1, other arithmetic: none -> 3.75 us  [per_device(): group_grad = jnp.sum(lax.all_gather(kernel_part, 'sub'), axis=0) * factor]
    unnamed x21 -> x26, local copies, waits for them, and re-layouts: 5.57 us -> 6.52 us
  transfers between devices with their start and end apart: 9 -> 9, of which waited for: 6 -> 6; matrix products, arithmetic and copies ran while one was open for 8% -> 9% of each run, Pallas kernels for 0% -> 0%
where the time goes in v1:
time: 219 us; the launch traced here: 218 us
  waiting for transfers between devices  107 us (49%)
  starting transfers between devices  29 us (13%)
  blocking collectives  28.8 us (13%)
  matrix products  16.7 us (8%)
  local copies, waits for them, and re-layouts  15.1 us (7%)
  between operations  14.5 us (7%)
  other arithmetic  7.21 us (3%)
    psum x1, waiting for transfers between devices, per_device(): first_grad = lax.psum(first_part, ('grp', 'sub')) * factor  89.5 us
    all_gather x1, blocking collectives, per_device(): group_grad = jnp.sum(lax.all_gather(kernel_part, 'sub'), axis=0) * factor  28.8 us
    ppermute x2, starting transfers between devices, padded_2(): lax.ppermute(lax.slice_in_dim(block, block.shape[dim] - width, None, axis...  8.89 us
    conv_general_dilated x1, matrix products, weight_grad(): lax.conv_general_dilated(padded[None], deltas[None], (1, 1, 1), 'VALID',...  7.94 us
    ppermute x2, waiting for transfers between devices, padded_2(): lax.ppermute(lax.slice_in_dim(block, 0, width, axis=dim), axis, backward)  6.74 us
    unnamed x26, local copies, waits for them, and re-layouts  6.52 us
    all_to_all x1, starting transfers between devices, per_device(): lax.all_to_all(first_act, 'grp', split_axis=0, concat_axis=1, tiled=True)  5.42 us
    all_to_all x1, waiting for transfers between devices, per_device(): lax.all_to_all(first_act, 'grp', split_axis=0, concat_axis=1, tiled=True)  4.73 us
  transfers between devices with their start and end apart: 9, of which 6 were waited for; matrix products, arithmetic and copies ran while one was open for 9% of the time, Pallas kernels for 0%

profile of v1, /device:TPU:1, one launch (start us, length us, event | category | flops | bytes accessed | tf_op | source)
XLA Modules:
  0.0 218.1 jit_solution(13073905262246154458)
XLA Ops:
  7.2 1.0 copy.129
  8.3 1.9 multiply_convert_fusion.2
  10.1 0.8 copy.130
  10.9 5.4 %all-to-all-start = ((bf16[256,1,2,128]{3,2,1,0:T(2,128)(2,1)}), bf16[256,1,2,128]{3,2,1,0:T(2,128)(2,1)S(1)}, u32[]{:S(2)}, u32[]{:S(2)}) async-start(bf16[256,1,2,128]{3,2,1,0:T(2,128)(2,1)} %copy.130), calls=%async_computation | async-start | bytes 262144 | tf_op jit(solution)/shard_map/all_to_all | solution.py:85
  16.3 0.1 compare_convert_fusion
  16.4 4.7 %all-to-all-done = bf16[256,1,2,128]{3,2,1,0:T(2,128)(2,1)S(1)} async-done(((bf16[256,1,2,128]{3,2,1,0:T(2,128)(2,1)}), bf16[256,1,2,128]{3,2,1,0:T(2,128)(2,1)S(1)}, u32[]{:S(2)}, u32[]{:S(2)}) %all-to-all-start) | async-done | bytes 131104 | tf_op jit(solution)/shard_map/all_to_all | solution.py:85
  21.2 5.2 %collective-permute-start = (bf16[64,4,1,128]{3,0,1,2:T(8,128)(2,1)S(1)}, bf16[64,4,1,128]{3,0,1,2:T(8,128)(2,1)S(1)}, u32[]{:S(2)}, u32[]{:S(2)}) collective-permute-start(bf16[64,4,1,128]{3,0,1,2:T(8,128)(2,1)S(1)} %get-tuple-element.43), channel_id=1, source_target_pairs={{0,1},{1,2},{2,3},{4,5},{5,6},{6,7},{8,9},{9,10},{10,11},{12,13},{... | collective-permute-start | bytes 196616 | tf_op jit(solution)/shard_map/ppermute | solution.py:15
  26.4 1.9 collective-permute-start.1
  28.3 0.1 constant_dynamic-slice_fusion
  28.5 3.5 %collective-permute-done.1 = bf16[64,4,1,128]{3,0,1,2:T(8,128)(2,1)S(1)} collective-permute-done((bf16[64,4,1,128]{3,0,1,2:T(8,128)(2,1)S(1)}, bf16[64,4,1,128]{3,0,1,2:T(8,128)(2,1)S(1)}, u32[]{:S(2)}, u32[]{:S(2)}) %collective-permute-start.1) | collective-permute-done | bytes 65568 | tf_op jit(solution)/shard_map/ppermute | solution.py:18
  32.0 0.3 copy.168
  32.4 0.3 pad.5.clone
  32.7 0.1 copy.134
  32.8 0.3 copy-done.7
  33.0 1.2 add_multiply_fusion
  34.3 0.3 copy.135
  34.6 0.2 copy.166
  34.8 0.7 fusion.28
  35.6 3.3 %all-to-all-start.1 = ((bf16[64,4,2,128]{3,0,2,1:T(8,128)(2,1)}), bf16[64,4,2,128]{3,0,2,1:T(8,128)(2,1)S(1)}, u32[]{:S(2)}, u32[]{:S(2)}) async-start(bf16[64,4,2,128]{3,0,2,1:T(8,128)(2,1)} %fusion.28), calls=%async_computation.1 | async-start | bytes 262144 | tf_op jit(solution)/shard_map/all_to_all | solution.py:89
  38.9 0.8 copy.138
  39.7 0.3 copy.150
  40.1 0.2 copy.167
  40.2 0.2 pad_bitcast_fusion
  40.5 1.7 copy.152
  42.2 1.4 all-to-all-done.1
  43.6 0.1 copy.137
  43.8 1.3 fusion.24
  45.1 0.8 copy.156
  45.9 0.2 convolution_convert_fusion
  46.1 0.8 copy.139
  46.9 3.3 %all-to-all-start.2 = ((bf16[256,1,2,128]{3,2,1,0:T(2,128)(2,1)}), bf16[256,1,2,128]{3,2,1,0:T(2,128)(2,1)S(1)}, u32[]{:S(2)}, u32[]{:S(2)}) async-start(bf16[256,1,2,128]{3,2,1,0:T(2,128)(2,1)} %copy.139), calls=%async_computation.2 | async-start | bytes 262144 | tf_op jit(solution)/shard_map/all_to_all | solution.py:107
  50.2 0.9 fusion.35
  51.1 4.3 %all-to-all-done.2 = bf16[256,1,2,128]{3,2,1,0:T(2,128)(2,1)S(1)} async-done(((bf16[256,1,2,128]{3,2,1,0:T(2,128)(2,1)}), bf16[256,1,2,128]{3,2,1,0:T(2,128)(2,1)S(1)}, u32[]{:S(2)}, u32[]{:S(2)}) %all-to-all-start.2) | async-done | bytes 131104 | tf_op jit(solution)/shard_map/all_to_all | solution.py:107
  55.5 0.1 fusion.23
  55.6 3.7 %collective-permute-start.2 = (bf16[64,4,1,128]{3,0,2,1:T(8,128)(2,1)S(1)}, bf16[64,4,1,128]{3,0,2,1:T(8,128)(2,1)S(1)}, u32[]{:S(2)}, u32[]{:S(2)}) collective-permute-start(bf16[64,4,1,128]{3,0,2,1:T(8,128)(2,1)S(1)} %get-tuple-element.41), channel_id=1, source_target_pairs={{0,1},{1,2},{2,3},{4,5},{5,6},{6,7},{8,9},{9,10},{10,11},{12,13},{... | collective-permute-start | bytes 196616 | tf_op jit(solution)/shard_map/ppermute | solution.py:15
  59.3 1.9 collective-permute-start.3
  61.2 0.4 copy.153
  61.7 3.2 %collective-permute-done.3 = bf16[64,4,1,128]{3,0,2,1:T(8,128)(2,1)S(1)} collective-permute-done((bf16[64,4,1,128]{3,0,2,1:T(8,128)(2,1)S(1)}, bf16[64,4,1,128]{3,0,2,1:T(8,128)(2,1)S(1)}, u32[]{:S(2)}, u32[]{:S(2)}) %collective-permute-start.3) | collective-permute-done | bytes 65568 | tf_op jit(solution)/shard_map/ppermute | solution.py:18
  64.9 0.3 copy.169
  65.2 0.3 pad.7.clone
  65.5 0.1 copy.144
  65.6 2.1 fusion.4
  67.7 0.2 copy.145
  67.9 0.2 slice_bitcast_fusion
  68.1 0.8 copy.146
  68.9 3.9 %all-to-all-start.3 = ((bf16[64,4,2,128]{3,0,2,1:T(8,128)(2,1)}), bf16[64,4,2,128]{3,0,2,1:T(8,128)(2,1)}, u32[]{:S(2)}, u32[]{:S(2)}) async-start(bf16[64,4,2,128]{3,0,2,1:T(8,128)(2,1)} %copy.146), calls=%async_computation.3 | async-start | bytes 262144 | tf_op jit(solution)/shard_map/all_to_all | solution.py:114
  72.9 0.2 all-reduce.4.cloned.1.call-start
  73.1 7.9 %fusion.3 = f32[8,64,3,3,3]{1,0,4,3,2:T(8,128)S(1)} fusion(bf16[1,64,6,4,130]{1,0,4,3,2:T(2,128)(2,1)S(1)} %copy.152, bf16[1,64,4,2,128]{1,0,4,3,2:T(2,128)(2,1)S(1)} %copy.153, f32[8,64]{1,0:T(8,128)S(1)} %fusion.40), kind=kOutput, calls=%fused_computation.7 | convolution fusion | flops 226699776 | bytes 587776 | tf_op jit(solution)/shard_map/conv_general_dilated | solution.py:59
  81.0 0.4 copy.154
  81.5 28.8 %all-gather = f32[256,8,3,3,3]{1,4,3,2,0:T(4,128)} all-gather(f32[64,8,3,3,3]{1,4,3,2,0:T(4,128)S(1)} %copy.154), channel_id=2, replica_groups=mesh['rep'=2,'grp'=4,'sub'=4] {'sub'}, dimensions={0}, use_global_device_ids=true | all-gather | bytes 276480 | tf_op jit(solution)/shard_map/all_gather | solution.py:115
  110.3 3.7 %reduce_sum.19 = f32[64,8,3,3,3]{1,4,3,2,0:T(4,128)S(1)} reduce(f32[4,64,8,3,3,3]{2,5,4,3,1,0:T(4,128)} %bitcast.136, f32[]{:T(128)} %constant.46.clone.1), dimensions={0}, to_apply=%region_2.3 | reduce | flops 41472 | bytes 276484 | tf_op jit(solution)/shard_map/reduce_sum | solution.py:115
  114.1 1.0 convert_bitcast_fusion
  115.1 0.2 copy.162
  115.3 0.3 reshape.179
  115.7 0.1 multiply_convert_fusion
  115.8 0.9 convolution_bitcast_fusion.1
  116.8 0.3 broadcast_multiply_fusion
  117.0 0.9 copy.159
  118.0 0.2 fusion.7
  118.2 0.8 copy.157
  119.0 89.5 %all-reduce.4.cloned.1.call-done = (f32[256,256]{0,1:T(8,128)}, f32[256,256]{0,1:T(8,128)}) async-done(((f32[256,256]{0,1:T(8,128)}, f32[256,256]{0,1:T(8,128)}), (f32[256,256]{0,1:T(8,128)}, f32[256,256]{0,1:T(8,128)})) %all-reduce.4.cloned.1.call-update) | async-done | bytes 524304 | tf_op jit(solution)/shard_map/psum | solution.py:130
  208.5 1.1 broadcast_multiply_fusion.1
  209.6 0.8 copy.160
  210.4 0.8 copy.158
  (32 shorter events, 0.4 us)
Async XLA Ops:
  7.2 36.6 %copy-start = (bf16[256,256]{1,0:T(8,128)(2,1)S(1)}, bf16[256,256]{1,0:T(8,128)(2,1)}, u32[]{:S(2)}) copy-start(bf16[256,256]{1,0:T(8,128)(2,1)} %param.9) | copy-start | bytes 393220
  8.2 35.5 %copy-start.1 = (bf16[256,1,2,128]{0,3,2,1:T(8,128)(2,1)}, bf16[256,1,2,128]{0,3,2,1:T(8,128)(2,1)S(1)}, u32[]{:S(2)}) copy-start(bf16[256,1,2,128]{0,3,2,1:T(8,128)(2,1)S(1)} %copy.129) | copy-start | bytes 393220
  8.2 20.1 %copy-start.6 = (bf16[256,8,3,3,3]{0,1,4,3,2:T(8,128)(2,1)S(1)}, bf16[256,8,3,3,3]{0,1,4,3,2:T(8,128)(2,1)}, u32[]{:S(2)}) copy-start(bf16[256,8,3,3,3]{0,1,4,3,2:T(8,128)(2,1)} %param.8) | copy-start | bytes 331780
  10.9 10.2 %all-to-all-start = ((bf16[256,1,2,128]{3,2,1,0:T(2,128)(2,1)}), bf16[256,1,2,128]{3,2,1,0:T(2,128)(2,1)S(1)}, u32[]{:S(2)}, u32[]{:S(2)}) async-start(bf16[256,1,2,128]{3,2,1,0:T(2,128)(2,1)} %copy.130), calls=%async_computation | async-start | bytes 262144 | tf_op jit(solution)/shard_map/all_to_all | solution.py:85
  21.2 7.3 %collective-permute-start = (bf16[64,4,1,128]{3,0,1,2:T(8,128)(2,1)S(1)}, bf16[64,4,1,128]{3,0,1,2:T(8,128)(2,1)S(1)}, u32[]{:S(2)}, u32[]{:S(2)}) collective-permute-start(bf16[64,4,1,128]{3,0,1,2:T(8,128)(2,1)S(1)} %get-tuple-element.43), channel_id=1, source_target_pairs={{0,1},{1,2},{2,3},{4,5},{5,6},{6,7},{8,9},{9,10},{10,11},{12,13},{... | collective-permute-start | bytes 196616 | tf_op jit(solution)/shard_map/ppermute | solution.py:15
  26.4 5.6 %collective-permute-start.1 = (bf16[64,4,1,128]{3,0,1,2:T(8,128)(2,1)S(1)}, bf16[64,4,1,128]{3,0,1,2:T(8,128)(2,1)S(1)}, u32[]{:S(2)}, u32[]{:S(2)}) collective-permute-start(bf16[64,4,1,128]{3,0,1,2:T(8,128)(2,1)S(1)} %get-tuple-element.44), channel_id=1, source_target_pairs={{1,0},{2,1},{3,2},{5,4},{6,5},{7,6},{9,8},{10,9},{11,10},{13,12},{... | collective-permute-start | bytes 196616 | tf_op jit(solution)/shard_map/ppermute | solution.py:18
  32.4 0.7 copy-start.7
  34.6 4.3 %copy-start.4 = (bf16[256,1,2,128]{3,2,1,0:T(2,128)(2,1)S(1)}, bf16[256,1,2,128]{3,2,1,0:T(2,128)(2,1)}, u32[]{:S(2)}) copy-start(bf16[256,1,2,128]{3,2,1,0:T(2,128)(2,1)} %param.6) | copy-start | bytes 393220
  35.6 8.1 %all-to-all-start.1 = ((bf16[64,4,2,128]{3,0,2,1:T(8,128)(2,1)}), bf16[64,4,2,128]{3,0,2,1:T(8,128)(2,1)S(1)}, u32[]{:S(2)}, u32[]{:S(2)}) async-start(bf16[64,4,2,128]{3,0,2,1:T(8,128)(2,1)} %fusion.28), calls=%async_computation.1 | async-start | bytes 262144 | tf_op jit(solution)/shard_map/all_to_all | solution.py:89
  46.9 8.6 %all-to-all-start.2 = ((bf16[256,1,2,128]{3,2,1,0:T(2,128)(2,1)}), bf16[256,1,2,128]{3,2,1,0:T(2,128)(2,1)S(1)}, u32[]{:S(2)}, u32[]{:S(2)}) async-start(bf16[256,1,2,128]{3,2,1,0:T(2,128)(2,1)} %copy.139), calls=%async_computation.2 | async-start | bytes 262144 | tf_op jit(solution)/shard_map/all_to_all | solution.py:107
  55.6 6.0 %collective-permute-start.2 = (bf16[64,4,1,128]{3,0,2,1:T(8,128)(2,1)S(1)}, bf16[64,4,1,128]{3,0,2,1:T(8,128)(2,1)S(1)}, u32[]{:S(2)}, u32[]{:S(2)}) collective-permute-start(bf16[64,4,1,128]{3,0,2,1:T(8,128)(2,1)S(1)} %get-tuple-element.41), channel_id=1, source_target_pairs={{0,1},{1,2},{2,3},{4,5},{5,6},{6,7},{8,9},{9,10},{10,11},{12,13},{... | collective-permute-start | bytes 196616 | tf_op jit(solution)/shard_map/ppermute | solution.py:15
  59.3 5.6 %collective-permute-start.3 = (bf16[64,4,1,128]{3,0,2,1:T(8,128)(2,1)S(1)}, bf16[64,4,1,128]{3,0,2,1:T(8,128)(2,1)S(1)}, u32[]{:S(2)}, u32[]{:S(2)}) collective-permute-start(bf16[64,4,1,128]{3,0,2,1:T(8,128)(2,1)S(1)} %get-tuple-element.42), channel_id=1, source_target_pairs={{1,0},{2,1},{3,2},{5,4},{6,5},{7,6},{9,8},{10,9},{11,10},{13,12},{... | collective-permute-start | bytes 196616 | tf_op jit(solution)/shard_map/ppermute | solution.py:18
  68.9 45.2 %all-to-all-start.3 = ((bf16[64,4,2,128]{3,0,2,1:T(8,128)(2,1)}), bf16[64,4,2,128]{3,0,2,1:T(8,128)(2,1)}, u32[]{:S(2)}, u32[]{:S(2)}) async-start(bf16[64,4,2,128]{3,0,2,1:T(8,128)(2,1)} %copy.146), calls=%async_computation.3 | async-start | bytes 262144 | tf_op jit(solution)/shard_map/all_to_all | solution.py:114
  72.9 135.6 %all-reduce.4.cloned.1.call-start = ((), (), s32[]{:S(2)}) async-start(), calls=%async_computation.4 | async-start | bytes 1048576 | tf_op jit(solution)/shard_map/psum | solution.py:130
  114.1 1.6 copy-start.3
  114.1 1.7 copy-start.2
  116.8 1.2 copy-start.5
Sparse Core Ops, SparseCore 0:
  116.9 91.5 all-reduce.3
